TPU v7x, 256 devices: a whole 4x4x8 slice. The times are simulated.
256 devices in a mesh: tensor: 2 (over core), row: 16 (over x, y), col: 8 (over z).
Axes of the slice: x: 4, y: 4, z: 8, core: 2. Of those that a mesh axis runs over, the one named last changes fastest.
Arguments:
- integral_tiles: bfloat16 [8192, 8, 4096], P(('tensor', 'row', 'col')), may hold values from -6 to 6
- tile_index: int32 [8192, 3], P(('tensor', 'row', 'col')), may hold values from 0 to 127, as said below
- virtual_coeff: bfloat16 [8192, 2048], P('col'), may hold values from -0.09375 to 0.09375
- occupied_coeff: bfloat16 [2048, 512], P('row'), may hold values from -0.125 to 0.125
Outputs:
- pair_tensor: bfloat16 [2048, 32, 512], P(('row', 'col'), 'tensor')
Inputs may be any that keep to these rules, and one draw needn't show every extreme that they name: `tile_index`: the tiles of the device at index (t, r, c) of tensor, row, col all have their nu block in c * 16 .. (c + 1) * 16 - 1, their auxiliary block below 4 and their mu block below 32. A tile's owner is (tensor index a // 2, row index m // 2) in the same col. Each device holds at most 2 tiles for any one owner; in every draw some owner gets exactly 2 tiles from every device of its col. Tiles with equal indices may occur and add up.
All inputs are finite; a program needn't handle non-finite values.
Results may differ from a plain program's by a relative error of at most 0.025.
Values may be sent and summed in bfloat16 or wider, within the bound.
No kernel may reach another device: no remote copies, remote signals or barrier semaphores. Data moves between devices by JAX's collectives and lax.ppermute only.
A program may use at most 128 MiB of HBM per device.

v0:
```python
import jax
import jax.numpy as jnp
from jax import lax
from jax.sharding import PartitionSpec as P

TB = 64
PB = 8
AB = 2
MB = 2
NBC = 16
CAP = 2
NV = 2048
NOCC = 512


def shards(integral_tiles, tile_index, virtual_coeff, occupied_coeff):
    tensor_at = lax.axis_index("tensor")
    row_at = lax.axis_index("row")
    col_at = lax.axis_index("col")
    tensor_count = lax.axis_size("tensor")
    row_count = lax.axis_size("row")
    col_count = lax.axis_size("col")
    held = integral_tiles.shape[0]
    aux_blocks = tensor_count * AB
    mu_blocks = row_count * MB
    quarters = tensor_count * 2
    qsize = TB // quarters
    assert row_count == 2 * PB and quarters * qsize == TB
    tiles = integral_tiles.reshape(held, PB, 2, tensor_count, qsize, TB)
    send = tiles.transpose(3, 1, 2, 0, 4, 5).reshape(tensor_count * row_count, held, qsize * TB)
    recv = lax.all_to_all(send, ("tensor", "row"), split_axis=0, concat_axis=0, tiled=True)
    recv = recv.reshape(tensor_count * row_count * held, qsize * TB)
    index = lax.all_gather(tile_index, ("tensor", "row"), axis=0, tiled=True)
    local_nu = index[:, 2] - col_at * NBC
    block = (index[:, 0] * NBC + local_nu) * mu_blocks + index[:, 1]
    blocks = aux_blocks * NBC * mu_blocks
    selector = (jnp.arange(blocks)[:, None] == block[None, :]).astype(jnp.bfloat16)
    dense = jnp.dot(selector, recv, preferred_element_type=jnp.float32).astype(jnp.bfloat16)
    dense = dense.reshape(aux_blocks, NBC, mu_blocks, qsize, TB)
    occ_all = lax.all_gather(occupied_coeff, "row", axis=0, tiled=True)
    quarter = 2 * (row_at % 2) + tensor_at
    occ_q = lax.dynamic_index_in_dim(
        occ_all.reshape(mu_blocks, quarters, qsize, NOCC), quarter, axis=1, keepdims=False
    )
    partial = jnp.einsum("anmuw,mui->anwi", dense, occ_q, preferred_element_type=jnp.float32)
    pair = lax.psum_scatter(partial.astype(jnp.bfloat16), "tensor", scatter_dimension=0, tiled=True)
    side = row_at % 2
    keep = lax.dynamic_index_in_dim(pair, side, axis=0, keepdims=False)
    give = lax.dynamic_index_in_dim(pair, 1 - side, axis=0, keepdims=False)
    got = lax.ppermute(give, "row", perm=[(i, i ^ 1) for i in range(row_count)])
    occ_done = (keep.astype(jnp.float32) + got.astype(jnp.float32)).astype(jnp.bfloat16)
    chunk = NV // (row_count * col_count)
    virt = virtual_coeff.reshape(NBC, TB, row_count, col_count, chunk)
    z = jnp.einsum("nwi,nwrcj->crji", occ_done, virt, preferred_element_type=jnp.float32)
    z = z.astype(jnp.bfloat16).reshape(col_count * row_count * chunk, NOCC)
    w = lax.psum_scatter(z, "col", scatter_dimension=0, tiled=True).reshape(row_count, chunk, NOCC)
    got_rows = lax.all_to_all(w, "row", split_axis=0, concat_axis=0, tiled=True)
    out = got_rows.reshape(PB, 2, chunk, NOCC).transpose(2, 1, 0, 3)
    return out.reshape(chunk, AB * PB, NOCC)


def solution(mesh):
    in_specs = (
        P(("tensor", "row", "col"), None, None),
        P(("tensor", "row", "col"), None),
        P("col", None),
        P("row", None),
    )
    out_specs = P(("row", "col"), "tensor", None)
    return jax.shard_map(shards, mesh=mesh, in_specs=in_specs, out_specs=out_specs, check_vma=False)
```

profile of v0, /device:TPU:32, one launch (start us, length us, event | category | flops | bytes accessed | tf_op | source)
XLA Modules:
  0.0 265.2 jit_solution(8073186442823905420)
XLA Ops:
  6.5 0.7 all-gather.3.cloned.1.call-update
  7.3 6.9 %reshape.57 = bf16[32,8,2,2,16,64]{5,4,3,2,1,0:T(8,128)(2,1)} reshape(bf16[32,8,4096]{2,1,0:T(8,128)(2,1)} %param.4) | data formatting | bytes 4194304 | tf_op jit(solution)/shard_map/reshape | solution.py:29
  14.2 5.3 %copy.42 = bf16[32,8,2,2,16,64]{5,4,0,2,1,3:T(8,128)(2,1)} copy(bf16[32,8,2,2,16,64]{5,4,3,2,1,0:T(8,128)(2,1)} %reshape.57) | data formatting | bytes 4194304 | tf_op jit(solution)/shard_map/reshape | solution.py:29
  19.5 6.5 %reshape.58 = bf16[32,32,1024]{2,1,0:T(8,128)(2,1)} reshape(bf16[2,8,2,32,16,64]{5,4,3,2,1,0:T(8,128)(2,1)} %bitcast.55) | data formatting | bytes 4194304 | tf_op jit(solution)/shard_map/reshape | solution.py:30
  26.0 7.3 %all-to-all-start = ((bf16[32,32,1024]{2,1,0:T(8,128)(2,1)}), bf16[32,32,1024]{2,1,0:T(8,128)(2,1)S(1)}, u32[]{:S(2)}, u32[]{:S(2)}) async-start(bf16[32,32,1024]{2,1,0:T(8,128)(2,1)} %reshape.58), calls=%async_computation | async-start | bytes 4194304 | tf_op jit(solution)/shard_map/all_to_all | solution.py:31
  33.4 0.0 reduce-scatter.3.cloned.1.call-start
  33.5 86.8 %all-gather = s32[32,32,3]{1,2,0:T(4,128)S(1)} all-gather(s32[1,32,3]{1,2,0:T(4,128)S(1)} %bitcast.62), channel_id=1, replica_groups=mesh['tensor'=2,'row'=16,'col'=8] {'tensor','row'}, dimensions={0}, use_global_device_ids=true | all-gather | bytes 12672 | tf_op jit(solution)/shard_map/all_gather | solution.py:33
  120.3 0.1 reshape.69
  120.4 6.0 %fusion.4 = bf16[2048,1024]{1,0:T(8,128)(2,1)} fusion(bf16[1024,1024]{1,0:T(8,128)(2,1)S(1)} %bitcast.57, s32[1024]{0:T(1024)S(1)} %bitcast.61), kind=kOutput, calls=%fused_computation.8 | convolution fusion | flops 4299161600 | bytes 6295552 | tf_op jit(solution)/shard_map/dot_general | solution.py:38
  126.4 11.6 %reshape.60 = bf16[4,16,32,16,64]{4,3,2,1,0:T(8,128)(2,1)} reshape(bf16[2048,1024]{1,0:T(8,128)(2,1)} %fusion.4) | data formatting | bytes 8388608 | tf_op jit(solution)/shard_map/reshape | solution.py:39
  138.0 7.8 %bitcast_convert_fusion = bf16[4,16,64,512]{3,2,1,0:T(8,128)(2,1)} fusion(bf16[4,16,32,16,64]{4,3,2,1,0:T(8,128)(2,1)} %reshape.60, bf16[32,4,16,512]{3,2,1,0:T(8,128)(2,1)} %bitcast.60, s32[]{:T(128)S(6)} %select_n.21), kind=kOutput, calls=%fused_computation | convolution fusion | flops 2149580800 | bytes 13107204 | tf_op jit(solution)/shard_map/anmuw,mui->anwi/dot_general | solution.py:45
  145.8 0.0 reduce-scatter.3.cloned.1.call-update
  145.8 0.0 reduce-scatter.5.cloned.1.call-start
  145.9 17.0 %reduce-scatter.3.cloned.1.call-done = bf16[2,16,64,512]{3,2,1,0:T(8,128)(2,1)} async-done(((bf16[4,16,64,512]{3,2,1,0:T(8,128)(2,1)}), bf16[2,16,64,512]{3,2,1,0:T(8,128)(2,1)}) %reduce-scatter.3.cloned.1.call-update) | async-done | bytes 2097168 | tf_op jit(solution)/shard_map/reduce_scatter | solution.py:46
  162.9 1.3 dynamic-slice_bitcast_fusion
  164.2 1.7 collective-permute-start
  165.9 6.4 %copy.25 = bf16[1024,2048]{0,1:T(8,128)(2,1)} copy(bf16[1024,2048]{1,0:T(8,128)(2,1)} %param.6) | data formatting | bytes 8388608 | tf_op args[2]
  172.3 11.8 %reshape.62 = bf16[16,64,16,8,16]{1,0,4,3,2:T(8,128)(2,1)} reshape(bf16[1024,2048]{0,1:T(8,128)(2,1)} %copy.25) | data formatting | bytes 8388608 | tf_op jit(solution)/shard_map/reshape | solution.py:53
  184.1 5.8 %collective-permute-done = bf16[16,64,512]{2,1,0:T(8,128)(2,1)} collective-permute-done((bf16[16,64,512]{2,1,0:T(8,128)(2,1)S(1)}, bf16[16,64,512]{2,1,0:T(8,128)(2,1)}, u32[]{:S(2)}, u32[]{:S(2)}) %collective-permute-start) | collective-permute-done | bytes 1048608 | tf_op jit(solution)/shard_map/ppermute | solution.py:50
  189.8 8.0 %fusion.8 = bf16[8,16,16,512]{3,2,0,1:T(8,128)(2,1)S(1)} fusion(bf16[16,64,16,8,16]{1,0,4,3,2:T(8,128)(2,1)} %reshape.62, bf16[16,64,512]{2,1,0:T(8,128)(2,1)} %collective-permute-done, bf16[2,16,64,512]{3,2,1,0:T(8,128)(2,1)S(1)} %copy-done, s32[]{:T(128)S(6)} %select_n.22), kind=kOutput, calls=%fused_computation.11 | convolution fusion | flops 2150629376 | bytes 8388612 | tf_op jit(solution)/shard_map/nwi,nwrcj->crji/dot_general | solution.py:54
  197.8 1.5 copy.27
  199.4 42.9 %reduce-scatter.5.cloned.1.call-done = bf16[256,512]{1,0:T(8,128)(2,1)} async-done(((bf16[2048,512]{1,0:T(8,128)(2,1)}), bf16[256,512]{1,0:T(8,128)(2,1)}) %reduce-scatter.5.cloned.1.call-update) | async-done | bytes 262160 | tf_op jit(solution)/shard_map/reduce_scatter | solution.py:56
  242.3 15.5 %all_to_all.10 = bf16[16,16,512]{2,1,0:T(8,128)(2,1)S(1)} all-to-all(bf16[16,16,512]{2,1,0:T(8,128)(2,1)} %bitcast.59), channel_id=1, replica_groups=mesh['tensor'=2,'row'=16,'col'=8] {'row'}, dimensions={0} | all-to-all | bytes 524288 | tf_op jit(solution)/shard_map/all_to_all | solution.py:57
  257.8 0.9 copy.43
  (10 shorter events, 0.1 us)
Async XLA Ops:
  6.5 131.5 %all-gather.3.cloned.1.call-start = ((), (), s32[]{:S(2)}) async-start(), calls=%async_computation.4 | async-start | bytes 2228224 | tf_op jit(solution)/shard_map/all_gather | solution.py:40
  19.5 13.9 %copy-start.1 = (s32[32,3]{0,1:T(4,128)S(1)}, s32[32,3]{0,1:T(4,128)}, u32[]{:S(2)}) copy-start(s32[32,3]{0,1:T(4,128)} %param.5) | copy-start | bytes 1156
  26.0 94.3 %all-to-all-start = ((bf16[32,32,1024]{2,1,0:T(8,128)(2,1)}), bf16[32,32,1024]{2,1,0:T(8,128)(2,1)S(1)}, u32[]{:S(2)}, u32[]{:S(2)}) async-start(bf16[32,32,1024]{2,1,0:T(8,128)(2,1)} %reshape.58), calls=%async_computation | async-start | bytes 4194304 | tf_op jit(solution)/shard_map/all_to_all | solution.py:31
  33.4 129.5 %reduce-scatter.3.cloned.1.call-start = ((), (), s32[]{:S(2)}) async-start(), calls=%async_computation.5 | async-start | bytes 6291456 | tf_op jit(solution)/shard_map/reduce_scatter | solution.py:46
  145.8 96.5 %reduce-scatter.5.cloned.1.call-start = ((), (), s32[]{:S(2)}) async-start(), calls=%async_computation.6 | async-start | bytes 2359296 | tf_op jit(solution)/shard_map/reduce_scatter | solution.py:56
  164.2 25.6 %collective-permute-start = (bf16[16,64,512]{2,1,0:T(8,128)(2,1)S(1)}, bf16[16,64,512]{2,1,0:T(8,128)(2,1)}, u32[]{:S(2)}, u32[]{:S(2)}) collective-permute-start(bf16[16,64,512]{2,1,0:T(8,128)(2,1)S(1)} %dynamic-slice_bitcast_fusion), channel_id=1, source_target_pairs={{0,8},{8,0},{16,24},{24,16},{32,40},{40,32},{48,56},{56,48},{64,72... | collective-permute-start | bytes 3145736 | tf_op jit(solution)/shard_map/ppermute | solution.py:50
  172.3 17.5 %copy-start = (bf16[2,16,64,512]{3,2,1,0:T(8,128)(2,1)S(1)}, bf16[2,16,64,512]{3,2,1,0:T(8,128)(2,1)}, u32[]{:S(2)}) copy-start(bf16[2,16,64,512]{3,2,1,0:T(8,128)(2,1)} %reduce-scatter.3.cloned.1.call-done) | copy-start | bytes 6291460
Sparse Core Ops, SparseCore 0:
  9.8 63.4 all-gather.2
  145.9 16.8 reduce-scatter.2
  199.5 42.7 reduce-scatter.4
where the time goes:
time: 266 us; the launch traced here: 265 us
  blocking collectives  102 us (38%)
  waiting for transfers between devices  66.4 us (25%)
  local copies, waits for them, and re-layouts  52.3 us (20%)
  matrix products  21.8 us (8%)
  between operations  13.2 us (5%)
  starting transfers between devices  9.15 us (3%)
    all_gather x1, blocking collectives, shards(): index = lax.all_gather(tile_index, ('tensor', 'row'), axis=0, tiled=True)  86.8 us
    reduce_scatter x1, waiting for transfers between devices, shards(): lax.psum_scatter(z, 'col', scatter_dimension=0, tiled=True)  42.9 us
    reduce_scatter x1, waiting for transfers between devices, shards(): lax.psum_scatter(partial.astype(jnp.bfloat16), 'tensor', scatter_dimensio...  17 us
    all_to_all x1, blocking collectives, shards(): got_rows = lax.all_to_all(w, 'row', split_axis=0, concat_axis=0, tiled=True)  15.5 us
    reshape x2, local copies, waits for them, and re-layouts, shards(): tiles = integral_tiles.reshape(held, PB, 2, tensor_count, qsize, TB)  12.3 us
    reshape x1, local copies, waits for them, and re-layouts, shards(): virt = virtual_coeff.reshape(NBC, TB, row_count, col_count, chunk)  11.8 us
    reshape x1, local copies, waits for them, and re-layouts, shards(): dense = dense.reshape(aux_blocks, NBC, mu_blocks, qsize, TB)  11.6 us
    dot_general x1, matrix products, shards(): jnp.einsum('nwi,nwrcj->crji', occ_done, virt, preferred_element_type=jnp....  7.97 us
  transfers between devices with their start and end apart: 5, of which 3 were waited for; matrix products, arithmetic and copies ran while one was open for 21% of the time, Pallas kernels for 0%

commit v1 on v0

--- a/solution.py
+++ b/solution.py
@@ -30,7 +30,12 @@
     send = tiles.transpose(3, 1, 2, 0, 4, 5).reshape(tensor_count * row_count, held, qsize * TB)
     recv = lax.all_to_all(send, ("tensor", "row"), split_axis=0, concat_axis=0, tiled=True)
     recv = recv.reshape(tensor_count * row_count * held, qsize * TB)
-    index = lax.all_gather(tile_index, ("tensor", "row"), axis=0, tiled=True)
+    index = jnp.concatenate(
+        lax.all_to_all(
+            jnp.stack([tile_index] * lax.axis_size(("tensor", "row"))), ("tensor", "row"), 0, 0
+        ),
+        axis=0,
+    )
     local_nu = index[:, 2] - col_at * NBC
     block = (index[:, 0] * NBC + local_nu) * mu_blocks + index[:, 1]
     blocks = aux_blocks * NBC * mu_blocks

time: 266 us -> 225 us (0.85)
  blocking collectives: 102 us -> 15.2 us
  waiting for transfers between devices: 66.4 us -> 104 us
  starting transfers between devices: 9.15 us -> 16.5 us
    all_gather x1 -> x0, blocking collectives: 86.8 us -> none  [shards(): index = lax.all_gather(tile_index, ('tensor', 'row'), axis=0, tiled=True)]
    all_to_all x1, waiting for transfers between devices: 0.01 us -> 35.3 us  [shards(): lax.all_to_all(send, ('tensor', 'row'), split_axis=0, concat_axis=0, tile...]
    all_to_all x0 -> x1, starting transfers between devices: none -> 7.32 us  [shards(): lax.all_to_all(jnp.stack([tile_index] * lax.axis_size(('tensor', 'row')))...]
    unnamed x6 -> x3, local copies, waits for them, and re-layouts: 6.47 us -> 6.4 us
  transfers between devices with their start and end apart: 5 -> 6, of which waited for: 3 -> 4; matrix products, arithmetic and copies ran while one was open for 21% -> 25% of each run, Pallas kernels for 0% -> 0%
where the time goes in v1:
time: 225 us; the launch traced here: 224 us
  waiting for transfers between devices  104 us (46%)
  local copies, waits for them, and re-layouts  53.7 us (24%)
  matrix products  21.8 us (10%)
  starting transfers between devices  16.5 us (7%)
  blocking collectives  15.2 us (7%)
  between operations  13.2 us (6%)
    reduce_scatter x1, waiting for transfers between devices, shards(): lax.psum_scatter(z, 'col', scatter_dimension=0, tiled=True)  43.2 us
    all_to_all x1, waiting for transfers between devices, shards(): lax.all_to_all(send, ('tensor', 'row'), split_axis=0, concat_axis=0, tile...  35.3 us
    reduce_scatter x1, waiting for transfers between devices, shards(): lax.psum_scatter(partial.astype(jnp.bfloat16), 'tensor', scatter_dimensio...  18.6 us
    all_to_all x1, blocking collectives, shards(): got_rows = lax.all_to_all(w, 'row', split_axis=0, concat_axis=0, tiled=True)  15.2 us
    reshape x2, local copies, waits for them, and re-layouts, shards(): tiles = integral_tiles.reshape(held, PB, 2, tensor_count, qsize, TB)  12.3 us
    reshape x1, local copies, waits for them, and re-layouts, shards(): virt = virtual_coeff.reshape(NBC, TB, row_count, col_count, chunk)  11.7 us
    reshape x1, local copies, waits for them, and re-layouts, shards(): dense = dense.reshape(aux_blocks, NBC, mu_blocks, qsize, TB)  11.6 us
    dot_general x1, matrix products, shards(): jnp.einsum('nwi,nwrcj->crji', occ_done, virt, preferred_element_type=jnp....  7.97 us
  transfers between devices with their start and end apart: 6, of which 4 were waited for; matrix products, arithmetic and copies ran while one was open for 25% of the time, Pallas kernels for 0%

profile of v1, /device:TPU:32, one launch (start us, length us, event | category | flops | bytes accessed | tf_op | source)
XLA Modules:
  0.0 223.9 jit_solution(2024560122701207661)
XLA Ops:
  6.5 0.7 all-gather.2.cloned.1.call-update
  7.3 1.3 stack.2
  8.6 7.3 %all-to-all-start = ((s32[32,32,3]{1,2,0:T(4,128)}), s32[32,32,3]{1,2,0:T(4,128)S(1)}, u32[]{:S(2)}, u32[]{:S(2)}) async-start(s32[32,32,3]{1,2,0:T(4,128)} %stack.2), calls=%async_computation | async-start | bytes 131072 | tf_op jit(solution)/shard_map/all_to_all | solution.py:34
  15.9 6.9 %reshape.63 = bf16[32,8,2,2,16,64]{5,4,3,2,1,0:T(8,128)(2,1)} reshape(bf16[32,8,4096]{2,1,0:T(8,128)(2,1)} %param.4) | data formatting | bytes 4194304 | tf_op jit(solution)/shard_map/reshape | solution.py:29
  22.8 5.4 %copy.47 = bf16[32,8,2,2,16,64]{5,4,0,2,1,3:T(8,128)(2,1)} copy(bf16[32,8,2,2,16,64]{5,4,3,2,1,0:T(8,128)(2,1)} %reshape.63) | data formatting | bytes 4194304 | tf_op jit(solution)/shard_map/reshape | solution.py:29
  28.2 6.5 %reshape.64 = bf16[32,32,1024]{2,1,0:T(8,128)(2,1)} reshape(bf16[2,8,2,32,16,64]{5,4,3,2,1,0:T(8,128)(2,1)} %bitcast.54) | data formatting | bytes 4194304 | tf_op jit(solution)/shard_map/reshape | solution.py:30
  34.7 7.4 %all-to-all-start.1 = ((bf16[32,32,1024]{2,1,0:T(8,128)(2,1)}), bf16[32,32,1024]{2,1,0:T(8,128)(2,1)S(1)}, u32[]{:S(2)}, u32[]{:S(2)}) async-start(bf16[32,32,1024]{2,1,0:T(8,128)(2,1)} %reshape.64), calls=%async_computation.1 | async-start | bytes 4194304 | tf_op jit(solution)/shard_map/all_to_all | solution.py:31
  42.1 0.0 reduce-scatter.3.cloned.1.call-start
  42.2 0.1 reshape.62
  42.3 35.3 %all-to-all-done.1 = bf16[32,32,1024]{2,1,0:T(8,128)(2,1)S(1)} async-done(((bf16[32,32,1024]{2,1,0:T(8,128)(2,1)}), bf16[32,32,1024]{2,1,0:T(8,128)(2,1)S(1)}, u32[]{:S(2)}, u32[]{:S(2)}) %all-to-all-start.1) | async-done | bytes 2097184 | tf_op jit(solution)/shard_map/all_to_all | solution.py:31
  77.7 6.0 %fusion.4 = bf16[2048,1024]{1,0:T(8,128)(2,1)} fusion(bf16[1024,1024]{1,0:T(8,128)(2,1)S(1)} %bitcast.56, s32[1024]{0:T(1024)S(1)} %bitcast.60), kind=kOutput, calls=%fused_computation.8 | convolution fusion | flops 4299161600 | bytes 6295552 | tf_op jit(solution)/shard_map/dot_general | solution.py:43
  83.7 11.6 %reshape.66 = bf16[4,16,32,16,64]{4,3,2,1,0:T(8,128)(2,1)} reshape(bf16[2048,1024]{1,0:T(8,128)(2,1)} %fusion.4) | data formatting | bytes 8388608 | tf_op jit(solution)/shard_map/reshape | solution.py:44
  95.3 7.8 %bitcast_convert_fusion = bf16[4,16,64,512]{3,2,1,0:T(8,128)(2,1)} fusion(bf16[4,16,32,16,64]{4,3,2,1,0:T(8,128)(2,1)} %reshape.66, bf16[32,4,16,512]{3,2,1,0:T(8,128)(2,1)} %bitcast.59, s32[]{:T(128)S(6)} %select_n.21), kind=kOutput, calls=%fused_computation | convolution fusion | flops 2149580800 | bytes 13107204 | tf_op jit(solution)/shard_map/anmuw,mui->anwi/dot_general | solution.py:50
  103.1 18.6 %reduce-scatter.3.cloned.1.call-done = bf16[2,16,64,512]{3,2,1,0:T(8,128)(2,1)} async-done(((bf16[4,16,64,512]{3,2,1,0:T(8,128)(2,1)}), bf16[2,16,64,512]{3,2,1,0:T(8,128)(2,1)}) %reduce-scatter.3.cloned.1.call-update) | async-done | bytes 2097168 | tf_op jit(solution)/shard_map/reduce_scatter | solution.py:51
  121.7 1.3 dynamic-slice_bitcast_fusion
  123.0 1.7 collective-permute-start
  124.8 6.4 %copy.30 = bf16[1024,2048]{0,1:T(8,128)(2,1)} copy(bf16[1024,2048]{1,0:T(8,128)(2,1)} %param.6) | data formatting | bytes 8388608 | tf_op args[2]
  131.2 11.7 %reshape.68 = bf16[16,64,16,8,16]{1,0,4,3,2:T(8,128)(2,1)} reshape(bf16[1024,2048]{0,1:T(8,128)(2,1)} %copy.30) | data formatting | bytes 8388608 | tf_op jit(solution)/shard_map/reshape | solution.py:58
  142.9 5.7 %collective-permute-done = bf16[16,64,512]{2,1,0:T(8,128)(2,1)} collective-permute-done((bf16[16,64,512]{2,1,0:T(8,128)(2,1)S(1)}, bf16[16,64,512]{2,1,0:T(8,128)(2,1)}, u32[]{:S(2)}, u32[]{:S(2)}) %collective-permute-start) | collective-permute-done | bytes 1048608 | tf_op jit(solution)/shard_map/ppermute | solution.py:55
  148.7 8.0 %fusion.8 = bf16[8,16,16,512]{3,2,0,1:T(8,128)(2,1)S(1)} fusion(bf16[16,64,16,8,16]{1,0,4,3,2:T(8,128)(2,1)} %reshape.68, bf16[16,64,512]{2,1,0:T(8,128)(2,1)} %collective-permute-done, bf16[2,16,64,512]{3,2,1,0:T(8,128)(2,1)S(1)} %copy-done, s32[]{:T(128)S(6)} %select_n.22), kind=kOutput, calls=%fused_computation.11 | convolution fusion | flops 2150629376 | bytes 8388612 | tf_op jit(solution)/shard_map/nwi,nwrcj->crji/dot_general | solution.py:59
  156.6 1.5 copy.32
  158.2 43.2 %reduce-scatter.5.cloned.1.call-done = bf16[256,512]{1,0:T(8,128)(2,1)} async-done(((bf16[2048,512]{1,0:T(8,128)(2,1)}), bf16[256,512]{1,0:T(8,128)(2,1)}) %reduce-scatter.5.cloned.1.call-update) | async-done | bytes 262160 | tf_op jit(solution)/shard_map/reduce_scatter | solution.py:61
  201.4 15.2 %all_to_all.15 = bf16[16,16,512]{2,1,0:T(8,128)(2,1)S(1)} all-to-all(bf16[16,16,512]{2,1,0:T(8,128)(2,1)} %bitcast.58), channel_id=1, replica_groups=mesh['tensor'=2,'row'=16,'col'=8] {'row'}, dimensions={0} | all-to-all | bytes 524288 | tf_op jit(solution)/shard_map/all_to_all | solution.py:62
  216.5 0.9 copy.48
  (10 shorter events, 0.1 us)
Async XLA Ops:
  6.5 88.7 %all-gather.2.cloned.1.call-start = ((), (), s32[]{:S(2)}) async-start(), calls=%async_computation.5 | async-start | bytes 2228224 | tf_op jit(solution)/shard_map/all_gather | solution.py:45
  8.6 26.1 %all-to-all-start = ((s32[32,32,3]{1,2,0:T(4,128)}), s32[32,32,3]{1,2,0:T(4,128)S(1)}, u32[]{:S(2)}, u32[]{:S(2)}) async-start(s32[32,32,3]{1,2,0:T(4,128)} %stack.2), calls=%async_computation | async-start | bytes 131072 | tf_op jit(solution)/shard_map/all_to_all | solution.py:34
  34.7 42.9 %all-to-all-start.1 = ((bf16[32,32,1024]{2,1,0:T(8,128)(2,1)}), bf16[32,32,1024]{2,1,0:T(8,128)(2,1)S(1)}, u32[]{:S(2)}, u32[]{:S(2)}) async-start(bf16[32,32,1024]{2,1,0:T(8,128)(2,1)} %reshape.64), calls=%async_computation.1 | async-start | bytes 4194304 | tf_op jit(solution)/shard_map/all_to_all | solution.py:31
  42.1 79.6 %reduce-scatter.3.cloned.1.call-start = ((), (), s32[]{:S(2)}) async-start(), calls=%async_computation.6 | async-start | bytes 6291456 | tf_op jit(solution)/shard_map/reduce_scatter | solution.py:51
  103.1 98.3 %reduce-scatter.5.cloned.1.call-start = ((), (), s32[]{:S(2)}) async-start(), calls=%async_computation.7 | async-start | bytes 2359296 | tf_op jit(solution)/shard_map/reduce_scatter | solution.py:61
  123.0 25.6 %collective-permute-start = (bf16[16,64,512]{2,1,0:T(8,128)(2,1)S(1)}, bf16[16,64,512]{2,1,0:T(8,128)(2,1)}, u32[]{:S(2)}, u32[]{:S(2)}) collective-permute-start(bf16[16,64,512]{2,1,0:T(8,128)(2,1)S(1)} %dynamic-slice_bitcast_fusion), channel_id=1, source_target_pairs={{0,8},{8,0},{16,24},{24,16},{32,40},{40,32},{48,56},{56,48},{64,72... | collective-permute-start | bytes 3145736 | tf_op jit(solution)/shard_map/ppermute | solution.py:55
  131.2 17.5 %copy-start = (bf16[2,16,64,512]{3,2,1,0:T(8,128)(2,1)S(1)}, bf16[2,16,64,512]{3,2,1,0:T(8,128)(2,1)}, u32[]{:S(2)}) copy-start(bf16[2,16,64,512]{3,2,1,0:T(8,128)(2,1)} %reduce-scatter.3.cloned.1.call-done) | copy-start | bytes 6291460
Sparse Core Ops, SparseCore 0:
  9.8 68.8 all-gather.1
  103.2 18.4 reduce-scatter.2
  158.3 43.0 reduce-scatter.4
